TPU v7x, 256 devices: a whole 4x4x8 slice. The times are simulated.
256 devices in a mesh: seq: 16 (over x_lo, y, core), chan: 16 (over x_hi, z).
Axes of the slice: x: 4 (x_hi: 2, x_lo: 2; x = x_hi * 2 + x_lo), y: 4, z: 8, core: 2. Of those that a mesh axis runs over, the one named last changes fastest.
Arguments:
- tokens: int32 [4096], P('seq'), may hold values from 0 to 511
- embedding: bfloat16 [512, 4096], P(None, 'chan'), may hold values from -6 to 6
- norm_gain: float32 [4096], replicated, may hold values from 0.5 to 1.5
- in_weight: bfloat16 [4096, 3, 4096], P(None, None, 'chan'), may hold values from -0.09375 to 0.09375
- short_filter: float32 [3, 3, 4096], P(None, None, 'chan'), may hold values from -3 to 3
- decay_rate: float32 [16, 4096], P(None, 'chan'), may hold values from 4.8828125e-06 to 0.025, as said below
- residue: float32 [16, 4096], P(None, 'chan'), may hold values from -0.06 to 0.06
- skip_gain: float32 [4096], P('chan'), may hold values from -4 to 4
- out_weight: bfloat16 [4096, 4096], P('chan'), may hold values from -0.125 to 0.125
Outputs:
- block_out: bfloat16 [4096, 4096], P('seq', 'chan')
Inputs may be any that keep to these rules, and one draw needn't show every extreme that they name: `decay_rate`: positive rates.
All inputs are finite; a program needn't handle non-finite values.
Results may differ from a plain program's by a relative error of at most 0.0091.
Values may be sent and summed in bfloat16 or wider, within the bound.
No kernel may reach another device: no remote copies, remote signals or barrier semaphores. Data moves between devices by JAX's collectives and lax.ppermute only.
A program may use at most 128 MiB of HBM per device.

v0:
```python
import jax
import jax.numpy as jnp
from jax import lax
from jax.sharding import PartitionSpec as P

FEAT = 3


def from_behind(value, axis, by):
    devices = lax.axis_size(axis)
    pairs = [(i, i + by) for i in range(devices) if 0 <= i + by < devices]
    return lax.ppermute(value, axis, pairs)


def on_device(
    tokens,
    embedding,
    norm_gain,
    in_weight,
    short_filter,
    decay_rate,
    residue,
    skip_gain,
    out_weight,
):
    token_rows = tokens.shape[0]
    vocab_size = embedding.shape[0]
    channels = embedding.shape[1]
    modes = decay_rate.shape[0]
    seq_devices = lax.axis_size("seq")
    place = lax.axis_index("seq")
    weight_cols = lax.all_to_all(out_weight, "chan", 1, 0, tiled=True)
    one_hot = (tokens[:, None] == jnp.arange(vocab_size, dtype=jnp.int32)[None, :]).astype(
        jnp.bfloat16
    )
    stream = jnp.dot(one_hot, embedding, preferred_element_type=jnp.float32).astype(jnp.bfloat16)
    gathered = lax.all_gather(stream, "chan", axis=1, tiled=True)
    gathered_f = gathered.astype(jnp.float32)
    scale = lax.rsqrt(jnp.mean(gathered_f * gathered_f, axis=1, keepdims=True) + 1e-06)
    normed = (gathered_f * scale * norm_gain[None, :]).astype(jnp.bfloat16)
    proj = jnp.einsum("td,djc->tjc", normed, in_weight, preferred_element_type=jnp.float32).astype(
        jnp.bfloat16
    )
    rim_rows = FEAT - 1
    earlier_rim = from_behind(proj[token_rows - rim_rows :], "seq", 1)
    padded = jnp.concatenate([earlier_rim, proj], axis=0).astype(jnp.float32)
    feat = short_filter[0][None] * padded[rim_rows : rim_rows + token_rows]
    for offset in range(1, FEAT):
        feat = (
            feat
            + short_filter[offset][None]
            * padded[rim_rows - offset : rim_rows - offset + token_rows]
        )
    feat = feat.astype(jnp.bfloat16)
    query = feat[:, 0].astype(jnp.float32)
    driven = feat[:, 1].astype(jnp.float32) * feat[:, 2].astype(jnp.float32)
    pos = jnp.arange(token_rows, dtype=jnp.float32)
    rise = jnp.exp(decay_rate[None] * pos[:, None, None])
    fall = residue[None] * jnp.exp(-decay_rate[None] * pos[:, None, None])
    rows = jnp.arange(token_rows)
    lower = (rows[:, None] >= rows[None, :]).astype(jnp.float32)
    lifted = rise * driven[:, None, :]
    running = jnp.dot(
        lower, lifted.reshape(token_rows, modes * channels), precision=lax.Precision.HIGHEST
    ).reshape(token_rows, modes, channels)
    local = jnp.sum(fall * running, axis=1)
    device_end = jnp.exp(-decay_rate * (token_rows - 1)) * jnp.sum(lifted, axis=0)
    ends = lax.all_gather(device_end, "seq")
    gap = place - 1 - jnp.arange(seq_devices)
    span = jnp.exp(
        -decay_rate[None] * (token_rows * jnp.maximum(gap, 0)).astype(jnp.float32)[:, None, None]
    )
    span = jnp.where((gap >= 0)[:, None, None], span, 0.0)
    incoming = jnp.sum(span * ends, axis=0) * jnp.exp(-decay_rate)
    carried = jnp.sum(fall * incoming[None], axis=1)
    long_out = local + carried + skip_gain[None, :] * driven
    hidden = (query * long_out).astype(jnp.bfloat16)
    hidden_all = lax.all_gather(hidden, "chan", axis=1, tiled=True)
    mixed = jnp.dot(hidden_all, weight_cols, preferred_element_type=jnp.float32)
    return (stream.astype(jnp.float32) + mixed).astype(jnp.bfloat16)


def solution(mesh):
    placed = (
        P("seq"),
        P(None, "chan"),
        P(),
        P(None, None, "chan"),
        P(None, None, "chan"),
        P(None, "chan"),
        P(None, "chan"),
        P("chan"),
        P("chan", None),
    )
    return jax.shard_map(
        on_device, mesh=mesh, in_specs=placed, out_specs=P("seq", "chan"), check_vma=False
    )
```

profile of v0, /device:TPU:8, one launch (start us, length us, event | category | flops | bytes accessed | tf_op | source)
XLA Modules:
  0.0 251.8 jit_solution(8482166742746502454)
XLA Ops:
  6.5 0.0 copy-start
  6.5 0.0 all-gather.4.cloned.1.call-start
  6.5 0.9 copy-done
  7.5 1.6 convolution_convert_fusion
  9.1 0.0 all-gather.4.cloned.1.call-update
  9.1 0.0 copy-start.3
  9.1 4.1 %copy.11 = bf16[256,4096]{0,1:T(8,128)(2,1)} copy(bf16[256,4096]{1,0:T(8,128)(2,1)} %param.17) | data formatting | bytes 4194304 | tf_op args[8]
  13.2 0.0 copy-start.5
  13.2 11.2 %all-to-all-start = ((bf16[256,16,256]{0,2,1:T(8,128)(2,1)}), bf16[256,16,256]{0,2,1:T(8,128)(2,1)S(1)}, u32[]{:S(2)}, u32[]{:S(2)}) async-start(bf16[256,16,256]{0,2,1:T(8,128)(2,1)} %bitcast.40), calls=%async_computation | async-start | bytes 4194304 | tf_op jit(solution)/shard_map/all_to_all | solution.py:32
  24.4 0.0 all-gather.6.cloned.1.call-start
  24.5 0.0 copy-done.3
  24.5 97.7 %all-gather.4.cloned.1.call-done = bf16[256,4096]{1,0:T(8,128)(2,1)} async-done(((bf16[256,256]{1,0:T(8,128)(2,1)}), bf16[256,4096]{1,0:T(8,128)(2,1)}) %all-gather.4.cloned.1.call-update) | async-done | bytes 2097168 | tf_op jit(solution)/shard_map/all_gather | solution.py:37
  122.2 2.1 fusion
  124.2 0.0 copy-done.5
  124.3 0.0 copy-start.1
  124.3 5.3 %fusion.8 = bf16[256,3,256]{2,0,1:T(8,128)(2,1)S(1)} fusion(bf16[4096,3,256]{2,0,1:T(8,128)(2,1)} %param.12, bf16[256,4096]{1,0:T(8,128)(2,1)} %all-gather.4.cloned.1.call-done, f32[4096]{0:T(1024)S(1)} %copy-done.5, f32[256]{0:T(256)S(1)} %add_rsqrt_fusion), kind=kOutput, calls=%fused_computation.14 | convolution fusion | flops 1615003648 | bytes 8799232 | tf_op jit(solution)/shard_map/td,djc->tjc/dot_general | solution.py:41
  129.6 1.9 collective-permute-start
  131.5 0.0 copy-done.1
  131.5 2.9 %collective-permute-done = bf16[2,3,256]{2,0,1:T(2,128)(2,1)S(1)} collective-permute-done((bf16[2,3,256]{2,0,1:T(2,128)(2,1)S(1)}, bf16[2,3,256]{2,0,1:T(2,128)(2,1)S(1)}, u32[]{:S(2)}, u32[]{:S(2)}) %collective-permute-start) | collective-permute-done | bytes 3104 | tf_op jit(solution)/shard_map/ppermute | solution.py:12
  134.5 0.1 maximum_convert_fusion
  134.6 0.3 fusion.13
  134.8 0.0 copy-start.6
  134.9 0.1 copy.10
  135.0 1.3 multiply_reduce_fusion.1
  136.4 16.6 %all-gather = f32[256,256]{1,0:T(8,128)S(1)} all-gather(f32[16,256]{1,0:T(8,128)S(1)} %get-tuple-element.5), channel_id=2, replica_groups=mesh['seq'=16,'chan'=16] {'seq'}, dimensions={0}, use_global_device_ids=true | all-gather | bytes 278528 | tf_op jit(solution)/shard_map/all_gather | solution.py:68
  153.0 0.1 multiply_reduce_fusion.3
  153.1 0.6 bitcast_multiply_fusion
  153.8 0.0 copy-done.6
  153.8 0.0 copy-start.4
  153.8 0.9 multiply_reduce_fusion
  154.7 3.3 %multiply_reduce_fusion.2 = f32[256,256]{1,0:T(8,128)S(1)} fusion(f32[16,256,256]{2,1,0:T(8,128)S(1)} %bitcast.41, f32[16,256]{1,0:T(8,128)S(1)} %get-tuple-element.6, f32[16,256]{1,0:T(8,128)S(1)} %copy-done.6), kind=kOutput, calls=%fused_computation.8 | convolution fusion | flops 3225419776 | bytes 4489216 | tf_op jit(solution)/shard_map/dot_general | solution.py:63
  157.9 0.0 copy-done.4
  157.9 0.0 copy-start.2
  157.9 0.7 fusion.15
  158.7 0.0 all-gather.6.cloned.1.call-update
  158.7 0.0 all-to-all-done
  158.7 2.4 copy.12
  161.1 80.3 %all-gather.6.cloned.1.call-done = bf16[256,4096]{1,0:T(8,128)(2,1)} async-done(((bf16[256,256]{1,0:T(8,128)(2,1)}), bf16[256,4096]{1,0:T(8,128)(2,1)}) %all-gather.6.cloned.1.call-update) | async-done | bytes 2097168 | tf_op jit(solution)/shard_map/all_gather | solution.py:78
  241.4 0.0 copy-done.2
  241.4 3.6 %fusion.11 = bf16[256,256]{1,0:T(8,128)(2,1)} fusion(bf16[256,4096]{1,0:T(8,128)(2,1)} %all-gather.6.cloned.1.call-done, bf16[4096,256]{1,0:T(8,128)(2,1)} %bitcast.42, bf16[256,256]{1,0:T(8,128)(2,1)S(1)} %copy-done.2), kind=kOutput, calls=%fused_computation.16 | convolution fusion | flops 537067520 | bytes 4456448 | tf_op jit(solution)/shard_map/dot_general | solution.py:79
  (9 shorter events, 0.1 us)
Async XLA Ops:
  6.5 1.0 copy-start
  6.5 115.6 %all-gather.4.cloned.1.call-start = ((), (), s32[]{:S(2)}) async-start(), calls=%async_computation.1 | async-start | bytes 2228224 | tf_op jit(solution)/shard_map/all_gather | solution.py:37
  9.1 15.3 %copy-start.3 = (f32[3,3,256]{2,1,0:T(4,128)S(1)}, f32[3,3,256]{2,1,0:T(4,128)}, u32[]{:S(2)}) copy-start(f32[3,3,256]{2,1,0:T(4,128)} %param.13) | copy-start | bytes 27652
  13.2 111.0 %copy-start.5 = (f32[4096]{0:T(1024)S(1)}, f32[4096]{0:T(1024)}, u32[]{:S(2)}) copy-start(f32[4096]{0:T(1024)} %param.11) | copy-start | bytes 49156
  13.2 145.5 %all-to-all-start = ((bf16[256,16,256]{0,2,1:T(8,128)(2,1)}), bf16[256,16,256]{0,2,1:T(8,128)(2,1)S(1)}, u32[]{:S(2)}, u32[]{:S(2)}) async-start(bf16[256,16,256]{0,2,1:T(8,128)(2,1)} %bitcast.40), calls=%async_computation | async-start | bytes 4194304 | tf_op jit(solution)/shard_map/all_to_all | solution.py:32
  24.4 217.0 %all-gather.6.cloned.1.call-start = ((), (), s32[]{:S(2)}) async-start(), calls=%async_computation.2 | async-start | bytes 2228224 | tf_op jit(solution)/shard_map/all_gather | solution.py:78
  124.3 7.3 %copy-start.1 = (f32[16,256]{1,0:T(8,128)S(1)}, f32[16,256]{1,0:T(8,128)}, u32[]{:S(2)}) copy-start(f32[16,256]{1,0:T(8,128)} %param.14) | copy-start | bytes 49156
  129.6 4.9 %collective-permute-start = (bf16[2,3,256]{2,0,1:T(2,128)(2,1)S(1)}, bf16[2,3,256]{2,0,1:T(2,128)(2,1)S(1)}, u32[]{:S(2)}, u32[]{:S(2)}) collective-permute-start(bf16[2,3,256]{2,0,1:T(2,128)(2,1)S(1)} %slice.40), channel_id=1, source_target_pairs={{0,16},{16,32},{32,48},{48,64},{64,80},{80,96},{96,112},{112,128},... | collective-permute-start | bytes 9224 | tf_op jit(solution)/shard_map/ppermute | solution.py:12
  134.8 18.9 %copy-start.6 = (f32[16,256]{1,0:T(8,128)S(1)}, f32[16,256]{1,0:T(8,128)}, u32[]{:S(2)}) copy-start(f32[16,256]{1,0:T(8,128)} %param.15) | copy-start | bytes 49156
  153.8 4.2 %copy-start.4 = (f32[256]{0:T(256)S(1)}, f32[256]{0:T(256)}, u32[]{:S(2)}) copy-start(f32[256]{0:T(256)} %param.16) | copy-start | bytes 3076
  157.9 83.5 %copy-start.2 = (bf16[256,256]{1,0:T(8,128)(2,1)S(1)}, bf16[256,256]{1,0:T(8,128)(2,1)}, u32[]{:S(2)}) copy-start(bf16[256,256]{1,0:T(8,128)(2,1)} %convolution_convert_fusion) | copy-start | bytes 393220
Sparse Core Ops, SparseCore 0:
  9.8 112.3 all-gather.3
  158.8 82.5 all-gather.5
where the time goes:
time: 252 us
  waiting for transfers between devices  181 us (72%)
  blocking collectives  16.6 us (7%)
  matrix products  13.7 us (5%)
  between operations  13.6 us (5%)
  starting transfers between devices  13.1 us (5%)
  local copies, waits for them, and re-layouts  7.62 us (3%)
  other arithmetic  6.17 us (2%)
    all_gather x1, waiting for transfers between devices, on_device(): gathered = lax.all_gather(stream, 'chan', axis=1, tiled=True)  97.7 us
    all_gather x1, waiting for transfers between devices, on_device(): hidden_all = lax.all_gather(hidden, 'chan', axis=1, tiled=True)  80.3 us
    all_gather x1, blocking collectives, on_device(): ends = lax.all_gather(device_end, 'seq')  16.6 us
    all_to_all x1, starting transfers between devices, on_device(): weight_cols = lax.all_to_all(out_weight, 'chan', 1, 0, tiled=True)  11.2 us
    dot_general x1, matrix products, on_device(): jnp.einsum('td,djc->tjc', normed, in_weight, preferred_element_type=jnp.f...  5.27 us
    unnamed x16, local copies, waits for them, and re-layouts  5.08 us
  transfers between devices with their start and end apart: 4, of which 3 were waited for; matrix products, arithmetic and copies ran while one was open for 8% of the time, Pallas kernels for 0%

commit v1 on v0

--- a/solution.py
+++ b/solution.py
@@ -75,7 +75,8 @@
     carried = jnp.sum(fall * incoming[None], axis=1)
     long_out = local + carried + skip_gain[None, :] * driven
     hidden = (query * long_out).astype(jnp.bfloat16)
-    hidden_all = lax.all_gather(hidden, "chan", axis=1, tiled=True)
+    sent = jnp.stack([hidden] * lax.axis_size("chan"))
+    hidden_all = jnp.concatenate(lax.all_to_all(sent, "chan", 0, 0), axis=1)
     mixed = jnp.dot(hidden_all, weight_cols, preferred_element_type=jnp.float32)
     return (stream.astype(jnp.float32) + mixed).astype(jnp.bfloat16)
 

time: 252 us -> 238 us (0.944)
  waiting for transfers between devices: 181 us -> 100 us
  blocking collectives: 16.6 us -> 73.7 us
  local copies, waits for them, and re-layouts: 7.62 us -> 16.6 us
    all_gather x1 -> x0, waiting for transfers between devices: 80.3 us -> none  [on_device(): hidden_all = lax.all_gather(hidden, 'chan', axis=1, tiled=True)]
    all_to_all x0 -> x1, blocking collectives: none -> 56.8 us  [on_device(): hidden_all = jnp.concatenate(lax.all_to_all(sent, 'chan', 0, 0), axis=1)]
    dot_general x0 -> x1, local copies, waits for them, and re-layouts: none -> 5.61 us  [on_device(): jnp.dot(lower, lifted.reshape(token_rows, modes * channels), precision=la...]
    unnamed x16 -> x19, local copies, waits for them, and re-layouts: 5.08 us -> 8.06 us
    dot_general x0 -> x1, other arithmetic: none -> 2.73 us  [on_device(): jnp.dot(lower, lifted.reshape(token_rows, modes * channels), precision=la...]
  transfers between devices with their start and end apart: 4 -> 3, of which waited for: 3 -> 2; matrix products, arithmetic and copies ran while one was open for 8% -> 13% of each run, Pallas kernels for 0% -> 0%
where the time goes in v1:
time: 238 us; the launch traced here: 236 us
  waiting for transfers between devices  100 us (42%)
  blocking collectives  73.7 us (31%)
  local copies, waits for them, and re-layouts  16.6 us (7%)
  between operations  13.6 us (6%)
  starting transfers between devices  13.1 us (6%)
  matrix products  11.5 us (5%)
  other arithmetic  7.02 us (3%)
    all_gather x1, waiting for transfers between devices, on_device(): gathered = lax.all_gather(stream, 'chan', axis=1, tiled=True)  97.3 us
    all_to_all x1, blocking collectives, on_device(): hidden_all = jnp.concatenate(lax.all_to_all(sent, 'chan', 0, 0), axis=1)  56.8 us
    all_gather x1, blocking collectives, on_device(): ends = lax.all_gather(device_end, 'seq')  16.9 us
    all_to_all x1, starting transfers between devices, on_device(): weight_cols = lax.all_to_all(out_weight, 'chan', 1, 0, tiled=True)  11.2 us
    unnamed x19, local copies, waits for them, and re-layouts  8.06 us
    dot_general x1, local copies, waits for them, and re-layouts, on_device(): jnp.dot(lower, lifted.reshape(token_rows, modes * channels), precision=la...  5.61 us
    dot_general x1, matrix products, on_device(): jnp.einsum('td,djc->tjc', normed, in_weight, preferred_element_type=jnp.f...  5.27 us
  transfers between devices with their start and end apart: 3, of which 2 were waited for; matrix products, arithmetic and copies ran while one was open for 13% of the time, Pallas kernels for 0%

profile of v1, /device:TPU:8, one launch (start us, length us, event | category | flops | bytes accessed | tf_op | source)
XLA Modules:
  0.0 235.9 jit_solution(4212927493994398202)
XLA Ops:
  6.5 0.0 copy-start
  6.5 0.0 all-gather.3.cloned.1.call-start
  6.5 0.9 copy-done
  7.5 1.6 convolution_convert_fusion
  9.1 0.0 all-gather.3.cloned.1.call-update
  9.1 3.3 %copy.15 = bf16[256,4096]{0,1:T(8,128)(2,1)S(1)} copy(bf16[256,4096]{1,0:T(8,128)(2,1)} %param.17) | data formatting | bytes 4194304 | tf_op args[8]
  12.4 0.0 copy-start.4
  12.4 2.4 %copy.16 = bf16[256,16,256]{2,0,1:T(8,128)(2,1)} copy(bf16[256,16,256]{0,2,1:T(8,128)(2,1)S(1)} %bitcast.61) | data formatting | bytes 4194304 | tf_op jit(solution)/shard_map/all_to_all | solution.py:32
  14.8 0.0 copy-start.6
  14.8 11.2 %all-to-all-start.1 = ((bf16[256,16,256]{2,0,1:T(8,128)(2,1)}), bf16[256,16,256]{2,0,1:T(8,128)(2,1)S(1)}, u32[]{:S(2)}, u32[]{:S(2)}) async-start(bf16[256,16,256]{2,0,1:T(8,128)(2,1)} %copy.16), calls=%async_computation.1 | async-start | bytes 4194304 | tf_op jit(solution)/shard_map/all_to_all | solution.py:32
  26.0 0.0 copy-done.4
  26.1 97.3 %all-gather.3.cloned.1.call-done = bf16[256,4096]{1,0:T(8,128)(2,1)} async-done(((bf16[256,256]{1,0:T(8,128)(2,1)}), bf16[256,4096]{1,0:T(8,128)(2,1)}) %all-gather.3.cloned.1.call-update) | async-done | bytes 2097168 | tf_op jit(solution)/shard_map/all_gather | solution.py:37
  123.3 2.1 fusion
  125.4 0.0 copy-done.6
  125.4 0.0 copy-start.2
  125.4 5.3 %fusion.11 = bf16[256,3,256]{2,0,1:T(8,128)(2,1)S(1)} fusion(bf16[4096,3,256]{2,0,1:T(8,128)(2,1)} %param.12, bf16[256,4096]{1,0:T(8,128)(2,1)} %all-gather.3.cloned.1.call-done, f32[4096]{0:T(1024)S(1)} %copy-done.6, f32[256]{0:T(256)S(1)} %add_rsqrt_fusion), kind=kOutput, calls=%fused_computation.17 | convolution fusion | flops 1615003648 | bytes 8799232 | tf_op jit(solution)/shard_map/td,djc->tjc/dot_general | solution.py:41
  130.7 1.9 collective-permute-start
  132.7 0.0 copy-done.2
  132.7 2.9 %collective-permute-done = bf16[2,3,256]{2,0,1:T(2,128)(2,1)S(1)} collective-permute-done((bf16[2,3,256]{2,0,1:T(2,128)(2,1)S(1)}, bf16[2,3,256]{2,0,1:T(2,128)(2,1)S(1)}, u32[]{:S(2)}, u32[]{:S(2)}) %collective-permute-start) | collective-permute-done | bytes 3104 | tf_op jit(solution)/shard_map/ppermute | solution.py:12
  135.6 0.1 maximum_convert_fusion
  135.7 0.3 fusion.30
  136.0 0.3 mul.200
  136.4 3.8 %copy.20 = f32[32,8,16,256]{3,1,2,0:T(8,128)S(1)} copy(f32[32,8,16,256]{3,2,1,0:T(8,128)S(1)} %bitcast.60) | data formatting | bytes 8388608
  140.2 2.7 %multiply_bitcast_fusion = f32[4096,256]{0,1:T(8,128)} fusion(f32[256,4096]{1,0:T(8,128)S(1)} %bitcast.59, f32[4096]{0:T(1024)S(1)} %bitcast.65), kind=kLoop, calls=%fused_computation.8 | loop fusion | flops 2097152 | bytes 8404992 | tf_op jit(solution)/shard_map/dot_general | solution.py:63
  142.9 0.0 copy-start.7
  142.9 5.6 %copy.12 = f32[4096,256]{1,0:T(8,128)} copy(f32[4096,256]{0,1:T(8,128)} %multiply_bitcast_fusion) | data formatting | bytes 8388608 | tf_op jit(solution)/shard_map/dot_general | solution.py:63
  148.5 0.0 copy-start.1
  148.5 0.7 multiply_reduce_fusion.1
  149.3 16.9 %all-gather = f32[256,256]{1,0:T(8,128)S(1)} all-gather(f32[16,256]{1,0:T(8,128)S(1)} %get-tuple-element.5), channel_id=2, replica_groups=mesh['seq'=16,'chan'=16] {'seq'}, dimensions={0}, use_global_device_ids=true | all-gather | bytes 278528 | tf_op jit(solution)/shard_map/all_gather | solution.py:68
  166.2 0.0 copy-start.5
  166.2 0.1 multiply_reduce_fusion.3
  166.3 0.0 copy-done.7
  166.4 0.9 multiply_reduce_fusion
  167.2 0.0 copy-done.1
  167.2 3.3 %multiply_reduce_fusion.2 = f32[256,256]{1,0:T(8,128)S(1)} fusion(f32[16,256,256]{2,1,0:T(8,128)S(1)} %bitcast.62, f32[16,256]{1,0:T(8,128)S(1)} %get-tuple-element.6, f32[16,256]{1,0:T(8,128)S(1)} %copy-done.7), kind=kOutput, calls=%fused_computation.7 | convolution fusion | flops 3225419776 | bytes 4489216 | tf_op jit(solution)/shard_map/dot_general | solution.py:63
  170.5 0.0 copy-done.5
  170.5 0.0 copy-start.3
  170.5 0.1 fusion.32
  170.6 0.0 all-to-all-done.1
  170.6 0.2 stack.2
  170.8 56.8 %all_to_all.21 = bf16[16,256,256]{2,1,0:T(8,128)(2,1)S(1)} all-to-all(bf16[16,256,256]{2,1,0:T(8,128)(2,1)S(1)} %stack.2), channel_id=1, replica_groups=mesh['seq'=16,'chan'=16] {'chan'}, dimensions={0} | all-to-all | bytes 4194304 | tf_op jit(solution)/shard_map/all_to_all | solution.py:79
  227.6 0.0 copy-done.3
  227.6 1.4 fusion.24
  (9 shorter events, 0.1 us)
Async XLA Ops:
  6.5 1.0 copy-start
  6.5 116.8 %all-gather.3.cloned.1.call-start = ((), (), s32[]{:S(2)}) async-start(), calls=%async_computation.2 | async-start | bytes 2228224 | tf_op jit(solution)/shard_map/all_gather | solution.py:37
  12.4 13.6 %copy-start.4 = (f32[3,3,256]{2,1,0:T(4,128)S(1)}, f32[3,3,256]{2,1,0:T(4,128)}, u32[]{:S(2)}) copy-start(f32[3,3,256]{2,1,0:T(4,128)} %param.13) | copy-start | bytes 27652
  14.8 110.6 %copy-start.6 = (f32[4096]{0:T(1024)S(1)}, f32[4096]{0:T(1024)}, u32[]{:S(2)}) copy-start(f32[4096]{0:T(1024)} %param.11) | copy-start | bytes 49156
  14.8 155.8 %all-to-all-start.1 = ((bf16[256,16,256]{2,0,1:T(8,128)(2,1)}), bf16[256,16,256]{2,0,1:T(8,128)(2,1)S(1)}, u32[]{:S(2)}, u32[]{:S(2)}) async-start(bf16[256,16,256]{2,0,1:T(8,128)(2,1)} %copy.16), calls=%async_computation.1 | async-start | bytes 4194304 | tf_op jit(solution)/shard_map/all_to_all | solution.py:32
  125.4 7.3 %copy-start.2 = (f32[16,256]{1,0:T(8,128)S(1)}, f32[16,256]{1,0:T(8,128)}, u32[]{:S(2)}) copy-start(f32[16,256]{1,0:T(8,128)} %param.14) | copy-start | bytes 49156
  130.7 4.9 %collective-permute-start = (bf16[2,3,256]{2,0,1:T(2,128)(2,1)S(1)}, bf16[2,3,256]{2,0,1:T(2,128)(2,1)S(1)}, u32[]{:S(2)}, u32[]{:S(2)}) collective-permute-start(bf16[2,3,256]{2,0,1:T(2,128)(2,1)S(1)} %slice.40), channel_id=1, source_target_pairs={{0,16},{16,32},{32,48},{48,64},{64,80},{80,96},{96,112},{112,128},... | collective-permute-start | bytes 9224 | tf_op jit(solution)/shard_map/ppermute | solution.py:12
  142.9 23.4 %copy-start.7 = (f32[16,256]{1,0:T(8,128)S(1)}, f32[16,256]{1,0:T(8,128)}, u32[]{:S(2)}) copy-start(f32[16,256]{1,0:T(8,128)} %param.15) | copy-start | bytes 49156
  148.5 18.7 %copy-start.1 = (f32[4096,256]{1,0:T(8,128)S(1)}, f32[4096,256]{1,0:T(8,128)}, u32[]{:S(2)}) copy-start(f32[4096,256]{1,0:T(8,128)} %copy.12) | copy-start | bytes 12582916
  166.2 4.3 %copy-start.5 = (f32[256]{0:T(256)S(1)}, f32[256]{0:T(256)}, u32[]{:S(2)}) copy-start(f32[256]{0:T(256)} %param.16) | copy-start | bytes 3076
  170.5 57.1 %copy-start.3 = (bf16[256,256]{1,0:T(8,128)(2,1)S(1)}, bf16[256,256]{1,0:T(8,128)(2,1)}, u32[]{:S(2)}) copy-start(bf16[256,256]{1,0:T(8,128)(2,1)} %convolution_convert_fusion) | copy-start | bytes 393220
Sparse Core Ops, SparseCore 0:
  9.8 113.4 all-gather.2
